TPU v7x, 32 devices: a whole 2x2x4 slice. The times are simulated.
32 devices in a mesh: dp: 8 (over y, x, core), tensor: 4 (over z).
Axes of the slice: x: 2, y: 2, z: 4, core: 2. Of those that a mesh axis runs over, the one named last changes fastest.
Arguments:
- acts: bfloat16 [4096, 2048], P('dp', 'tensor'), may hold values from -6 to 6
- out_grads: bfloat16 [4096, 8192], P('dp', 'tensor'), may hold values from -6 to 6
- basis_out: bfloat16 [8192, 8192], P('tensor'), may hold values from -0.0625 to 0.0625
- basis_in: bfloat16 [2048, 2048], P('tensor'), may hold values from -0.125 to 0.125
- slot_sequence: int32 [16], replicated, may hold values from 0 to 15, each once
- seq_lengths: int32 [16], replicated, may hold values from 1 to 256, 2560 in all
Outputs:
- eigenvalues: float32 [8192, 2048], P('tensor', 'dp')
Inputs may be any that keep to these rules, and one draw needn't show every extreme that they name: `slot_sequence`: every sequence number appears exactly once. `seq_lengths`: the largest count is exactly 256.
All inputs are finite; a program needn't handle non-finite values.
Results may differ from a plain program's by a relative error of at most 0.0018.
Values may be sent and summed in bfloat16 or wider, within the bound.
No kernel may reach another device: no remote copies, remote signals or barrier semaphores. Data moves between devices by JAX's collectives and lax.ppermute only.
A program may use at most 128 MiB of HBM per device.

v0:
```python
import jax
import jax.numpy as jnp
from jax import lax
from jax.sharding import PartitionSpec as P

LEN = 256
VALID_NUM, VALID_DEN = (5, 8)
CHUNKS = 4


def redistribute(x, dp):
    slots = x.shape[0] // LEN
    width = x.shape[1]
    x = x.reshape(slots, LEN // dp, dp, width).transpose(2, 0, 1, 3).reshape(-1, width)
    return lax.all_to_all(x, "dp", 0, 0, tiled=True)


def shards(acts, out_grads, basis_out, basis_in, slot_sequence, seq_lengths, *, dp, tp):
    tok_rows = acts.shape[0]
    nseq = seq_lengths.shape[0]
    per = LEN // dp
    total = nseq * LEN * VALID_NUM // VALID_DEN
    cap = -(-(total + nseq * (dp - 1)) // dp)
    cap = -(-cap // 16) * 16
    rows_all = dp * cap
    group = lax.axis_index("dp")
    counts = seq_lengths[slot_sequence]
    groups = jnp.arange(dp, dtype=jnp.int32)
    kept = jnp.clip((counts[:, None] - groups[None, :] + dp - 1) // dp, 0, per)
    ends = jnp.cumsum(kept, axis=0)
    starts = ends - kept
    my_ends = ends[:, group]
    my_starts = starts[:, group]
    rows = jnp.arange(cap, dtype=jnp.int32)
    slot_of = jnp.sum((my_ends[None, :] <= rows[:, None]).astype(jnp.int32), axis=1)
    in_use = slot_of < nseq
    slot_c = jnp.minimum(slot_of, nseq - 1)
    src = jnp.clip(slot_c * per + rows - my_starts[slot_c], 0, nseq * per - 1)
    grads_r = redistribute(out_grads, dp)
    grads_p = jnp.take(grads_r, src, axis=0, mode="clip")
    grads_p = jnp.where(in_use[:, None], grads_p, jnp.zeros_like(grads_p))
    acts_r = redistribute(acts, dp)
    acts_p = jnp.take(acts_r, src, axis=0, mode="clip")
    act_part = jnp.dot(acts_p, basis_in, preferred_element_type=jnp.float32)
    act_sum = lax.psum_scatter(act_part, "tensor", scatter_dimension=1, tiled=True)
    act_whole = lax.all_gather(act_sum.astype(jnp.bfloat16), "tensor", axis=1, tiled=True)
    in_cols = act_whole.shape[1] // dp
    act_whole = act_whole.reshape(cap, dp, in_cols).transpose(1, 0, 2).reshape(-1, in_cols)
    rot_acts = lax.all_to_all(act_whole, "dp", 0, 0, tiled=True)
    lo = groups[None, :] * cap + starts
    win = jnp.minimum(lo, rows_all - per)
    js = jnp.arange(per, dtype=jnp.int32)
    at = win[:, :, None] + js[None, None, :]
    live = (at >= lo[:, :, None]) & (at < (lo + kept)[:, :, None])

    def windows(rows_of, slot):
        return jnp.concatenate(
            [lax.dynamic_slice_in_dim(rows_of, win[slot, g], per, 0) for g in range(dp)]
        )

    units = cap // 16
    bounds = [16 * (c * units // CHUNKS) for c in range(CHUNKS + 1)]
    pieces = []
    for c in range(CHUNKS):
        if c == 1:
            grads_p, rot_acts = lax.optimization_barrier((grads_p, rot_acts))
        block = grads_p[bounds[c] : bounds[c + 1]]
        grad_part = jnp.dot(block, basis_out, preferred_element_type=jnp.float32)
        rot_grads = lax.psum_scatter(grad_part, "tensor", scatter_dimension=1, tiled=True)
        rot_grads = rot_grads.astype(jnp.bfloat16)
        sent = jnp.broadcast_to(rot_grads[None], (dp,) + rot_grads.shape).reshape(
            -1, rot_grads.shape[1]
        )
        got = lax.all_to_all(sent, "dp", 0, 0, tiled=True)
        pieces.append(got.reshape(dp, -1, got.shape[1]))
    all_grads = jnp.concatenate(pieces, axis=1).reshape(rows_all, -1)

    def one_slot(slot, squares):
        g_s = windows(all_grads, slot)
        a_s = windows(rot_acts, slot)
        a_s = jnp.where(live[slot].reshape(-1, 1), a_s, jnp.zeros_like(a_s))
        rotated = lax.dot_general(
            g_s, a_s, (((0,), (0,)), ((), ())), preferred_element_type=jnp.float32
        )
        return squares + rotated * rotated

    squares = jnp.zeros((all_grads.shape[1], rot_acts.shape[1]), jnp.float32)
    squares = lax.fori_loop(0, nseq, one_slot, squares)
    return squares / (nseq * LEN)


def solution(mesh):
    dp = mesh.shape["dp"]
    tp = mesh.shape["tensor"]

    def body(*args):
        return shards(*args, dp=dp, tp=tp)

    return jax.shard_map(
        body,
        mesh=mesh,
        in_specs=(
            P("dp", "tensor"),
            P("dp", "tensor"),
            P("tensor", None),
            P("tensor", None),
            P(),
            P(),
        ),
        out_specs=P("tensor", "dp"),
        check_vma=False,
    )
```

profile of v0, /device:TPU:0, one launch (start us, length us, event | category | flops | bytes accessed | tf_op | source)
XLA Modules:
  0.0 841.4 jit_solution(1465902554699397482)
XLA Ops:
  8.7 5.2 all-to-all-start.2
  17.2 4.3 fusion.22
  21.5 5.7 select_select_fusion
  35.8 4.1 all-to-all-start
  40.0 26.6 %all-to-all-done = bf16[8,64,2048]{2,1,0:T(8,128)(2,1)S(1)} async-done(((bf16[8,64,2048]{2,1,0:T(8,128)(2,1)}), bf16[8,64,2048]{2,1,0:T(8,128)(2,1)S(1)}, u32[]{:S(2)}, u32[]{:S(2)}) %all-to-all-start) | async-done | bytes 2097184 | tf_op jit(solution)/shard_map/all_to_all | solution.py:15
  69.0 18.9 %reduce-scatter.8.cloned.1.call-done = f32[336,512]{1,0:T(8,128)} async-done(((f32[336,2048]{1,0:T(8,128)}), f32[336,512]{1,0:T(8,128)}) %reduce-scatter.8.cloned.1.call-update) | async-done | bytes 688144 | tf_op jit(solution)/shard_map/reduce_scatter | solution.py:45
  90.0 15.4 %fusion.7 = f32[80,8192]{1,0:T(8,128)} fusion(bf16[2048,8192]{1,0:T(8,128)(2,1)} %param.10, bf16[336,2048]{1,0:T(8,128)(2,1)S(1)} %broadcast_select_fusion), kind=kOutput, calls=%fused_computation.40 | convolution fusion | flops 2684354560 | bytes 36503552 | tf_op jit(solution)/shard_map/dot_general | solution.py:68
  105.5 17.7 %all-gather.2.cloned.1.call-done = bf16[336,2048]{1,0:T(8,128)(2,1)} async-done(((bf16[336,512]{1,0:T(8,128)(2,1)}), bf16[336,2048]{1,0:T(8,128)(2,1)}) %all-gather.2.cloned.1.call-update) | async-done | bytes 1376272 | tf_op jit(solution)/shard_map/all_gather | solution.py:46
  124.7 22.3 %all_to_all.57 = bf16[8,336,256]{2,1,0:T(8,128)(2,1)S(1)} all-to-all(bf16[8,336,256]{2,1,0:T(8,128)(2,1)S(1)} %bitcast.72), channel_id=1, replica_groups=mesh['dp'=8,'tensor'=4] {'dp'}, dimensions={0} | all-to-all | bytes 2752512 | tf_op jit(solution)/shard_map/all_to_all | solution.py:49
  147.0 15.2 %fusion.11 = f32[80,8192]{1,0:T(8,128)} fusion(bf16[2048,8192]{1,0:T(8,128)(2,1)} %param.10, bf16[336,2048]{1,0:T(8,128)(2,1)S(1)} %broadcast_select_fusion), kind=kOutput, calls=%fused_computation.44 | convolution fusion | flops 2684354560 | bytes 36503552 | tf_op jit(solution)/shard_map/dot_general | solution.py:68
  162.5 15.2 %fusion.9 = f32[80,8192]{1,0:T(8,128)} fusion(bf16[2048,8192]{1,0:T(8,128)(2,1)} %param.10, bf16[336,2048]{1,0:T(8,128)(2,1)S(1)} %broadcast_select_fusion), kind=kOutput, calls=%fused_computation.42 | convolution fusion | flops 2684354560 | bytes 36503552 | tf_op jit(solution)/shard_map/dot_general | solution.py:68
  180.7 4.4 all-to-all-start.1
  185.2 15.1 %fusion.5 = f32[96,8192]{1,0:T(8,128)} fusion(bf16[2048,8192]{1,0:T(8,128)(2,1)} %param.10, bf16[336,2048]{1,0:T(8,128)(2,1)S(1)} %broadcast_select_fusion), kind=kOutput, calls=%fused_computation.38 | convolution fusion | flops 3221225472 | bytes 37093376 | tf_op jit(solution)/shard_map/dot_general | solution.py:68
  200.3 30.6 %reduce-scatter.10.cloned.1.call-done = f32[80,2048]{1,0:T(8,128)} async-done(((f32[80,8192]{1,0:T(8,128)}), f32[80,2048]{1,0:T(8,128)}) %reduce-scatter.10.cloned.1.call-update) | async-done | bytes 655376 | tf_op jit(solution)/shard_map/reduce_scatter | solution.py:69
  233.9 4.4 all-to-all-start.4
  238.2 46.6 %reduce-scatter.12.cloned.1.call-done = f32[80,2048]{1,0:T(8,128)} async-done(((f32[80,8192]{1,0:T(8,128)}), f32[80,2048]{1,0:T(8,128)}) %reduce-scatter.12.cloned.1.call-update) | async-done | bytes 655376 | tf_op jit(solution)/shard_map/reduce_scatter | solution.py:69
  287.9 4.4 all-to-all-start.5
  292.3 54.7 %reduce-scatter.14.cloned.1.call-done = f32[96,2048]{1,0:T(8,128)} async-done(((f32[96,8192]{1,0:T(8,128)}), f32[96,2048]{1,0:T(8,128)}) %reduce-scatter.14.cloned.1.call-update) | async-done | bytes 786448 | tf_op jit(solution)/shard_map/reduce_scatter | solution.py:69
  350.3 4.5 all-to-all-start.6
  354.9 37.6 %all-to-all-done.6 = bf16[8,96,2048]{2,1,0:T(8,128)(2,1)} async-done(((bf16[8,96,2048]{2,1,0:T(8,128)(2,1)}), bf16[8,96,2048]{2,1,0:T(8,128)(2,1)}, u32[]{:S(2)}, u32[]{:S(2)}) %all-to-all-start.6) | async-done | bytes 3145760 | tf_op jit(solution)/shard_map/all_to_all | solution.py:74
  392.6 10.6 %pad_maximum_fusion = bf16[8,336,2048]{2,1,0:T(8,128)(2,1)} fusion(bf16[8,96,2048]{2,1,0:T(8,128)(2,1)} %all-to-all-done.6, bf16[8,80,2048]{2,1,0:T(8,128)(2,1)} %all-to-all-done.5, bf16[8,80,2048]{2,1,0:T(8,128)(2,1)} %all-to-all-done.4, bf16[8,80,2048]{2,1,0:T(8,128)(2,1)} %all-to-all-done.1), kind=kLoop, calls=%fused_computation.34 | loop fusion | flops 44040192 | bytes 22020096 | tf_op jit(solution)/shard_map/concatenate | solution.py:76
  403.2 428.2 %while.14 = (s32[]{:T(128)}, f32[2048,256]{1,0:T(8,128)}, s32[16,8]{0,1:T(8,128)S(1)}, bf16[2688,2048]{1,0:T(8,128)(2,1)}, pred[16,8,32]{2,1,0:T(8,128)(4,1)S(1)...) while((s32[]{:T(128)}, f32[2048,256]{1,0:T(8,128)}, ...), condition=%wide.region_8.9_spmd.clone, body=%wide.region_7.8_spmd.clone.sunk | while | flops 270073888 | bytes 7735039 | solution.py:88
  478.7 3.5 fusion.38
  505.6 3.5 fusion.38
  532.4 3.5 fusion.38
  559.3 3.5 fusion.38
  586.2 3.5 fusion.38
  613.0 3.5 fusion.38
  639.9 3.5 fusion.38
  666.7 3.5 fusion.38
  693.6 3.5 fusion.38
  720.5 3.5 fusion.38
  (369 shorter events, 192.8 us)
Async XLA Ops:
  6.5 22.8 %copy-start = (bf16[512,2048]{1,0:T(8,128)(2,1)S(1)}, bf16[512,2048]{1,0:T(8,128)(2,1)}, u32[]{:S(2)}) copy-start(bf16[512,2048]{1,0:T(8,128)(2,1)} %param.11) | copy-start | bytes 6291460
  8.7 18.6 %all-to-all-start.2 = ((bf16[8,64,512]{2,1,0:T(8,128)(2,1)}), bf16[8,64,512]{2,1,0:T(8,128)(2,1)S(1)}, u32[]{:S(2)}, u32[]{:S(2)}) async-start(bf16[8,64,512]{2,1,0:T(8,128)(2,1)} %bitcast.22), calls=%async_computation.3 | async-start | bytes 1048576 | tf_op jit(solution)/shard_map/all_to_all | solution.py:15
  13.9 74.0 %reduce-scatter.8.cloned.1.call-start = ((), (), s32[]{:S(2)}) async-start(), calls=%async_computation.13 | async-start | bytes 3440640 | tf_op jit(solution)/shard_map/reduce_scatter | solution.py:45
  31.8 1.6 copy-start.2
  35.8 30.8 %all-to-all-start = ((bf16[8,64,2048]{2,1,0:T(8,128)(2,1)}), bf16[8,64,2048]{2,1,0:T(8,128)(2,1)S(1)}, u32[]{:S(2)}, u32[]{:S(2)}) async-start(bf16[8,64,2048]{2,1,0:T(8,128)(2,1)} %bitcast.71), calls=%async_computation | async-start | bytes 4194304 | tf_op jit(solution)/shard_map/all_to_all | solution.py:15
  40.0 83.3 %all-gather.2.cloned.1.call-start = ((), (), s32[]{:S(2)}) async-start(), calls=%async_computation.14 | async-start | bytes 1720320 | tf_op jit(solution)/shard_map/all_gather | solution.py:46
  89.8 87.9 %reduce-scatter.6.cloned.1.call-start = ((), (), s32[]{:S(2)}) async-start(), calls=%async_computation.12 | async-start | bytes 3276800 | tf_op jit(solution)/shard_map/reduce_scatter | solution.py:69
  105.5 125.4 %reduce-scatter.10.cloned.1.call-start = ((), (), s32[]{:S(2)}) async-start(), calls=%async_computation.15 | async-start | bytes 3276800 | tf_op jit(solution)/shard_map/reduce_scatter | solution.py:69
  162.2 122.7 %reduce-scatter.12.cloned.1.call-start = ((), (), s32[]{:S(2)}) async-start(), calls=%async_computation.16 | async-start | bytes 3276800 | tf_op jit(solution)/shard_map/reduce_scatter | solution.py:69
  180.7 51.3 %all-to-all-start.1 = ((bf16[8,80,2048]{2,1,0:T(8,128)(2,1)}), bf16[8,80,2048]{2,1,0:T(8,128)(2,1)}, u32[]{:S(2)}, u32[]{:S(2)}) async-start(bf16[8,80,2048]{2,1,0:T(8,128)(2,1)} %broadcast_in_dim.79), calls=%async_computation.2 | async-start | bytes 5242880 | tf_op jit(solution)/shard_map/all_to_all | solution.py:74
  185.2 161.9 %reduce-scatter.14.cloned.1.call-start = ((), (), s32[]{:S(2)}) async-start(), calls=%async_computation.17 | async-start | bytes 3932160 | tf_op jit(solution)/shard_map/reduce_scatter | solution.py:69
  233.9 52.2 %all-to-all-start.4 = ((bf16[8,80,2048]{2,1,0:T(8,128)(2,1)}), bf16[8,80,2048]{2,1,0:T(8,128)(2,1)}, u32[]{:S(2)}, u32[]{:S(2)}) async-start(bf16[8,80,2048]{2,1,0:T(8,128)(2,1)} %broadcast_in_dim.80), calls=%async_computation.7 | async-start | bytes 5242880 | tf_op jit(solution)/shard_map/all_to_all | solution.py:74
  287.9 60.3 %all-to-all-start.5 = ((bf16[8,80,2048]{2,1,0:T(8,128)(2,1)}), bf16[8,80,2048]{2,1,0:T(8,128)(2,1)}, u32[]{:S(2)}, u32[]{:S(2)}) async-start(bf16[8,80,2048]{2,1,0:T(8,128)(2,1)} %broadcast_in_dim.81), calls=%async_computation.9 | async-start | bytes 5242880 | tf_op jit(solution)/shard_map/all_to_all | solution.py:74
  350.3 42.3 %all-to-all-start.6 = ((bf16[8,96,2048]{2,1,0:T(8,128)(2,1)}), bf16[8,96,2048]{2,1,0:T(8,128)(2,1)}, u32[]{:S(2)}, u32[]{:S(2)}) async-start(bf16[8,96,2048]{2,1,0:T(8,128)(2,1)} %broadcast_in_dim.82), calls=%async_computation.11 | async-start | bytes 6291456 | tf_op jit(solution)/shard_map/all_to_all | solution.py:74
  831.4 3.2 copy-start.1
Sparse Core Ops, SparseCore 0:
  31.9 55.9 reduce-scatter.7
  89.9 33.2 all-gather.1
  125.6 51.2 reduce-scatter.5
  179.1 51.7 reduce-scatter.9
  233.0 51.7 reduce-scatter.11
  287.0 59.9 reduce-scatter.13
where the time goes:
time: 849 us; the launch traced here: 841 us
  loops' own time  237 us (28%)
  waiting for transfers between devices  233 us (27%)
  local copies, waits for them, and re-layouts  160 us (19%)
  matrix products  117 us (14%)
  other arithmetic  31.5 us (4%)
  starting transfers between devices  27.4 us (3%)
  blocking collectives  22.3 us (3%)
  between operations  13.7 us (2%)
    another operation x1, loops' own time, shards(): squares = lax.fori_loop(0, nseq, one_slot, squares)  237 us
    reduce_scatter x4, waiting for transfers between devices, shards(): lax.psum_scatter(grad_part, 'tensor', scatter_dimension=1, tiled=True)  132 us
    while x224, local copies, waits for them, and re-layouts  110 us
    dot_general x4, matrix products, shards(): grad_part = jnp.dot(block, basis_out, preferred_element_type=jnp.float32)  60.9 us
    dot_general x16, matrix products, one_slot(): lax.dot_general(g_s, a_s, (((0,), (0,)), ((), ())), preferred_element_typ...  53.7 us
    all_to_all x4, waiting for transfers between devices, shards(): got = lax.all_to_all(sent, 'dp', 0, 0, tiled=True)  37.7 us
    all_to_all x2, waiting for transfers between devices, redistribute(): return lax.all_to_all(x, 'dp', 0, 0, tiled=True)  26.6 us
    all_to_all x1, blocking collectives, shards(): rot_acts = lax.all_to_all(act_whole, 'dp', 0, 0, tiled=True)  22.3 us
  transfers between devices with their start and end apart: 12, of which 7 were waited for; matrix products, arithmetic and copies ran while one was open for 11% of the time, Pallas kernels for 0%

commit v1 on v0

--- a/solution.py
+++ b/solution.py
@@ -43,7 +43,16 @@
     acts_p = jnp.take(acts_r, src, axis=0, mode="clip")
     act_part = jnp.dot(acts_p, basis_in, preferred_element_type=jnp.float32)
     act_sum = lax.psum_scatter(act_part, "tensor", scatter_dimension=1, tiled=True)
-    act_whole = lax.all_gather(act_sum.astype(jnp.bfloat16), "tensor", axis=1, tiled=True)
+    shard = act_sum.astype(jnp.bfloat16)
+    ways, here, step = (lax.axis_size("tensor"), lax.axis_index("tensor"), shard.shape[1])
+    line, have = (shard, 1)
+    while have < ways:
+        line = jnp.concatenate(
+            [line, lax.ppermute(line, "tensor", [(d, (d - have) % ways) for d in range(ways)])],
+            axis=1,
+        )
+        have = 2 * have
+    act_whole = jnp.roll(line, here * step, axis=1)
     in_cols = act_whole.shape[1] // dp
     act_whole = act_whole.reshape(cap, dp, in_cols).transpose(1, 0, 2).reshape(-1, in_cols)
     rot_acts = lax.all_to_all(act_whole, "dp", 0, 0, tiled=True)

time: 849 us -> 881 us (1.038)
  waiting for transfers between devices: 233 us -> 258 us
    ppermute x0 -> x2, waiting for transfers between devices: none -> 76.5 us  [shards(): lax.ppermute(line, 'tensor', [(d, (d - have) % ways) for d in range(ways)])]
    reduce_scatter x4, waiting for transfers between devices: 132 us -> 111 us  [shards(): lax.psum_scatter(grad_part, 'tensor', scatter_dimension=1, tiled=True)]
    all_gather x1 -> x0, waiting for transfers between devices: 17.7 us -> none  [shards(): lax.all_gather(act_sum.astype(jnp.bfloat16), 'tensor', axis=1, tiled=True)]
    reduce_scatter x1, waiting for transfers between devices: 18.9 us -> 3.45 us  [shards(): lax.psum_scatter(act_part, 'tensor', scatter_dimension=1, tiled=True)]
  transfers between devices with their start and end apart: 12 -> 13, of which waited for: 7 -> 9; matrix products, arithmetic and copies ran while one was open for 11% -> 11% of each run, Pallas kernels for 0% -> 0%
where the time goes in v1:
time: 881 us; the launch traced here: 873 us
  waiting for transfers between devices  258 us (29%)
  loops' own time  237 us (27%)
  local copies, waits for them, and re-layouts  165 us (19%)
  matrix products  117 us (13%)
  other arithmetic  31.6 us (4%)
  starting transfers between devices  29.2 us (3%)
  blocking collectives  21.9 us (2%)
  between operations  13.4 us (2%)
    another operation x1, loops' own time, shards(): squares = lax.fori_loop(0, nseq, one_slot, squares)  237 us
    reduce_scatter x4, waiting for transfers between devices, shards(): lax.psum_scatter(grad_part, 'tensor', scatter_dimension=1, tiled=True)  111 us
    while x224, local copies, waits for them, and re-layouts  110 us
    ppermute x2, waiting for transfers between devices, shards(): lax.ppermute(line, 'tensor', [(d, (d - have) % ways) for d in range(ways)])  76.5 us
    dot_general x4, matrix products, shards(): grad_part = jnp.dot(block, basis_out, preferred_element_type=jnp.float32)  61 us
    dot_general x16, matrix products, one_slot(): lax.dot_general(g_s, a_s, (((0,), (0,)), ((), ())), preferred_element_typ...  53.8 us
    all_to_all x4, waiting for transfers between devices, shards(): got = lax.all_to_all(sent, 'dp', 0, 0, tiled=True)  40.7 us
    all_to_all x2, waiting for transfers between devices, redistribute(): return lax.all_to_all(x, 'dp', 0, 0, tiled=True)  26.6 us
  transfers between devices with their start and end apart: 13, of which 9 were waited for; matrix products, arithmetic and copies ran while one was open for 11% of the time, Pallas kernels for 0%

profile of v1, /device:TPU:0, one launch (start us, length us, event | category | flops | bytes accessed | tf_op | source)
XLA Modules:
  0.0 873.2 jit_solution(12375529929914311482)
XLA Ops:
  8.7 5.2 all-to-all-start.2
  17.2 4.3 fusion.22
  21.5 5.7 select_select_fusion
  35.8 4.1 all-to-all-start
  40.0 26.6 %all-to-all-done = bf16[8,64,2048]{2,1,0:T(8,128)(2,1)S(1)} async-done(((bf16[8,64,2048]{2,1,0:T(8,128)(2,1)}), bf16[8,64,2048]{2,1,0:T(8,128)(2,1)S(1)}, u32[]{:S(2)}, u32[]{:S(2)}) %all-to-all-start) | async-done | bytes 2097184 | tf_op jit(solution)/shard_map/all_to_all | solution.py:15
  69.2 15.2 %fusion.7 = f32[80,8192]{1,0:T(8,128)} fusion(bf16[2048,8192]{1,0:T(8,128)(2,1)} %param.10, bf16[336,2048]{1,0:T(8,128)(2,1)S(1)} %broadcast_select_fusion), kind=kOutput, calls=%fused_computation.40 | convolution fusion | flops 2684354560 | bytes 36503552 | tf_op jit(solution)/shard_map/dot_general | solution.py:77
  91.6 12.6 %collective-permute-done = bf16[336,512]{1,0:T(8,128)(2,1)S(1)} collective-permute-done((bf16[336,512]{1,0:T(8,128)(2,1)S(1)}, bf16[336,512]{1,0:T(8,128)(2,1)S(1)}, u32[]{:S(2)}, u32[]{:S(2)}) %collective-permute-start) | collective-permute-done | bytes 344096 | tf_op jit(solution)/shard_map/ppermute | solution.py:51
  105.2 63.9 %collective-permute-done.1 = bf16[336,1024]{1,0:T(8,128)(2,1)S(1)} collective-permute-done((bf16[336,1024]{1,0:T(8,128)(2,1)S(1)}, bf16[336,1024]{1,0:T(8,128)(2,1)S(1)}, u32[]{:S(2)}, u32[]{:S(2)}) %collective-permute-start.1) | collective-permute-done | bytes 688160 | tf_op jit(solution)/shard_map/ppermute | solution.py:51
  174.6 21.9 %all_to_all.57 = bf16[8,336,256]{2,1,0:T(8,128)(2,1)S(1)} all-to-all(bf16[8,336,256]{2,1,0:T(8,128)(2,1)S(1)} %copy.23), channel_id=1, replica_groups=mesh['dp'=8,'tensor'=4] {'dp'}, dimensions={0} | all-to-all | bytes 2752512 | tf_op jit(solution)/shard_map/all_to_all | solution.py:58
  196.6 15.1 %fusion.11 = f32[80,8192]{1,0:T(8,128)} fusion(bf16[2048,8192]{1,0:T(8,128)(2,1)} %param.10, bf16[336,2048]{1,0:T(8,128)(2,1)S(1)} %broadcast_select_fusion), kind=kOutput, calls=%fused_computation.44 | convolution fusion | flops 2684354560 | bytes 36503552 | tf_op jit(solution)/shard_map/dot_general | solution.py:77
  211.9 15.5 %fusion.9 = f32[80,8192]{1,0:T(8,128)} fusion(bf16[2048,8192]{1,0:T(8,128)(2,1)} %param.10, bf16[336,2048]{1,0:T(8,128)(2,1)S(1)} %broadcast_select_fusion), kind=kOutput, calls=%fused_computation.42 | convolution fusion | flops 2684354560 | bytes 36503552 | tf_op jit(solution)/shard_map/dot_general | solution.py:77
  230.5 4.4 all-to-all-start.1
  234.9 15.1 %fusion.5 = f32[96,8192]{1,0:T(8,128)} fusion(bf16[2048,8192]{1,0:T(8,128)(2,1)} %param.10, bf16[336,2048]{1,0:T(8,128)(2,1)S(1)} %broadcast_select_fusion), kind=kOutput, calls=%fused_computation.38 | convolution fusion | flops 3221225472 | bytes 37093376 | tf_op jit(solution)/shard_map/dot_general | solution.py:77
  250.1 12.9 %reduce-scatter.10.cloned.1.call-done = f32[80,2048]{1,0:T(8,128)} async-done(((f32[80,8192]{1,0:T(8,128)}), f32[80,2048]{1,0:T(8,128)}) %reduce-scatter.10.cloned.1.call-update) | async-done | bytes 655376 | tf_op jit(solution)/shard_map/reduce_scatter | solution.py:78
  269.0 4.4 all-to-all-start.4
  273.4 43.6 %reduce-scatter.12.cloned.1.call-done = f32[80,2048]{1,0:T(8,128)} async-done(((f32[80,8192]{1,0:T(8,128)}), f32[80,2048]{1,0:T(8,128)}) %reduce-scatter.12.cloned.1.call-update) | async-done | bytes 655376 | tf_op jit(solution)/shard_map/reduce_scatter | solution.py:78
  320.0 4.4 all-to-all-start.5
  324.4 54.7 %reduce-scatter.14.cloned.1.call-done = f32[96,2048]{1,0:T(8,128)} async-done(((f32[96,8192]{1,0:T(8,128)}), f32[96,2048]{1,0:T(8,128)}) %reduce-scatter.14.cloned.1.call-update) | async-done | bytes 786448 | tf_op jit(solution)/shard_map/reduce_scatter | solution.py:78
  382.4 4.5 all-to-all-start.6
  387.0 37.6 %all-to-all-done.6 = bf16[8,96,2048]{2,1,0:T(8,128)(2,1)} async-done(((bf16[8,96,2048]{2,1,0:T(8,128)(2,1)}), bf16[8,96,2048]{2,1,0:T(8,128)(2,1)}, u32[]{:S(2)}, u32[]{:S(2)}) %all-to-all-start.6) | async-done | bytes 3145760 | tf_op jit(solution)/shard_map/all_to_all | solution.py:83
  424.7 10.6 %pad_maximum_fusion = bf16[8,336,2048]{2,1,0:T(8,128)(2,1)} fusion(bf16[8,96,2048]{2,1,0:T(8,128)(2,1)} %all-to-all-done.6, bf16[8,80,2048]{2,1,0:T(8,128)(2,1)} %all-to-all-done.5, bf16[8,80,2048]{2,1,0:T(8,128)(2,1)} %all-to-all-done.4, bf16[8,80,2048]{2,1,0:T(8,128)(2,1)} %all-to-all-done.1), kind=kLoop, calls=%fused_computation.34 | loop fusion | flops 44040192 | bytes 22020096 | tf_op jit(solution)/shard_map/concatenate | solution.py:85
  435.3 428.2 %while.14 = (s32[]{:T(128)}, f32[2048,256]{1,0:T(8,128)}, s32[16,8]{0,1:T(8,128)S(1)}, bf16[2688,2048]{1,0:T(8,128)(2,1)}, pred[16,8,32]{2,1,0:T(8,128)(4,1)S(1)...) while((s32[]{:T(128)}, f32[2048,256]{1,0:T(8,128)}, ...), condition=%wide.region_8.9_spmd.clone, body=%wide.region_7.8_spmd.clone.sunk | while | flops 270073888 | bytes 7735039 | solution.py:97
  483.9 3.5 fusion.38
  510.8 3.5 fusion.38
  537.7 3.5 fusion.38
  564.5 3.5 fusion.38
  591.4 3.5 fusion.38
  645.1 3.5 fusion.38
  698.8 3.5 fusion.38
  752.6 3.5 fusion.38
  806.3 3.5 fusion.38
  860.0 3.5 fusion.38
  (378 shorter events, 206.1 us)
Async XLA Ops:
  6.5 22.8 %copy-start = (bf16[512,2048]{1,0:T(8,128)(2,1)S(1)}, bf16[512,2048]{1,0:T(8,128)(2,1)}, u32[]{:S(2)}) copy-start(bf16[512,2048]{1,0:T(8,128)(2,1)} %param.11) | copy-start | bytes 6291460
  8.7 18.6 %all-to-all-start.2 = ((bf16[8,64,512]{2,1,0:T(8,128)(2,1)}), bf16[8,64,512]{2,1,0:T(8,128)(2,1)S(1)}, u32[]{:S(2)}, u32[]{:S(2)}) async-start(bf16[8,64,512]{2,1,0:T(8,128)(2,1)} %bitcast.22), calls=%async_computation.3 | async-start | bytes 1048576 | tf_op jit(solution)/shard_map/all_to_all | solution.py:15
  13.9 74.0 %reduce-scatter.8.cloned.1.call-start = ((), (), s32[]{:S(2)}) async-start(), calls=%async_computation.13 | async-start | bytes 3440640 | tf_op jit(solution)/shard_map/reduce_scatter | solution.py:45
  31.8 1.6 copy-start.2
  35.8 30.8 %all-to-all-start = ((bf16[8,64,2048]{2,1,0:T(8,128)(2,1)}), bf16[8,64,2048]{2,1,0:T(8,128)(2,1)S(1)}, u32[]{:S(2)}, u32[]{:S(2)}) async-start(bf16[8,64,2048]{2,1,0:T(8,128)(2,1)} %bitcast.68), calls=%async_computation | async-start | bytes 4194304 | tf_op jit(solution)/shard_map/all_to_all | solution.py:15
  40.0 187.5 %reduce-scatter.6.cloned.1.call-start = ((), (), s32[]{:S(2)}) async-start(), calls=%async_computation.12 | async-start | bytes 3276800 | tf_op jit(solution)/shard_map/reduce_scatter | solution.py:78
  84.4 178.5 %reduce-scatter.10.cloned.1.call-start = ((), (), s32[]{:S(2)}) async-start(), calls=%async_computation.14 | async-start | bytes 3276800 | tf_op jit(solution)/shard_map/reduce_scatter | solution.py:78
  89.9 14.3 %collective-permute-start = (bf16[336,512]{1,0:T(8,128)(2,1)S(1)}, bf16[336,512]{1,0:T(8,128)(2,1)S(1)}, u32[]{:S(2)}, u32[]{:S(2)}) collective-permute-start(bf16[336,512]{1,0:T(8,128)(2,1)S(1)} %get-tuple-element.195), channel_id=1, source_target_pairs={{0,3},{1,0},{2,1},{3,2},{4,7},{5,4},{6,5},{7,6},{8,11},{9,8},{10,9... | collective-permute-start | bytes 1032200 | tf_op jit(solution)/shard_map/ppermute | solution.py:51
  104.3 64.8 %collective-permute-start.1 = (bf16[336,1024]{1,0:T(8,128)(2,1)S(1)}, bf16[336,1024]{1,0:T(8,128)(2,1)S(1)}, u32[]{:S(2)}, u32[]{:S(2)}) collective-permute-start(bf16[336,1024]{1,0:T(8,128)(2,1)S(1)} %pad_maximum_fusion.1), channel_id=1, source_target_pairs={{0,2},{1,3},{2,0},{3,1},{4,6},{5,7},{6,4},{7,5},{8,10},{9,11},{10,... | collective-permute-start | bytes 2064392 | tf_op jit(solution)/shard_map/ppermute | solution.py:51
  211.7 105.3 %reduce-scatter.12.cloned.1.call-start = ((), (), s32[]{:S(2)}) async-start(), calls=%async_computation.15 | async-start | bytes 3276800 | tf_op jit(solution)/shard_map/reduce_scatter | solution.py:78
  230.5 36.7 %all-to-all-start.1 = ((bf16[8,80,2048]{2,1,0:T(8,128)(2,1)}), bf16[8,80,2048]{2,1,0:T(8,128)(2,1)}, u32[]{:S(2)}, u32[]{:S(2)}) async-start(bf16[8,80,2048]{2,1,0:T(8,128)(2,1)} %broadcast_in_dim.79), calls=%async_computation.2 | async-start | bytes 5242880 | tf_op jit(solution)/shard_map/all_to_all | solution.py:83
  234.9 144.2 %reduce-scatter.14.cloned.1.call-start = ((), (), s32[]{:S(2)}) async-start(), calls=%async_computation.16 | async-start | bytes 3932160 | tf_op jit(solution)/shard_map/reduce_scatter | solution.py:78
  269.0 49.1 %all-to-all-start.4 = ((bf16[8,80,2048]{2,1,0:T(8,128)(2,1)}), bf16[8,80,2048]{2,1,0:T(8,128)(2,1)}, u32[]{:S(2)}, u32[]{:S(2)}) async-start(bf16[8,80,2048]{2,1,0:T(8,128)(2,1)} %broadcast_in_dim.80), calls=%async_computation.7 | async-start | bytes 5242880 | tf_op jit(solution)/shard_map/all_to_all | solution.py:83
  320.0 60.3 %all-to-all-start.5 = ((bf16[8,80,2048]{2,1,0:T(8,128)(2,1)}), bf16[8,80,2048]{2,1,0:T(8,128)(2,1)}, u32[]{:S(2)}, u32[]{:S(2)}) async-start(bf16[8,80,2048]{2,1,0:T(8,128)(2,1)} %broadcast_in_dim.81), calls=%async_computation.9 | async-start | bytes 5242880 | tf_op jit(solution)/shard_map/all_to_all | solution.py:83
  382.4 42.3 %all-to-all-start.6 = ((bf16[8,96,2048]{2,1,0:T(8,128)(2,1)}), bf16[8,96,2048]{2,1,0:T(8,128)(2,1)}, u32[]{:S(2)}, u32[]{:S(2)}) async-start(bf16[8,96,2048]{2,1,0:T(8,128)(2,1)} %broadcast_in_dim.82), calls=%async_computation.11 | async-start | bytes 6291456 | tf_op jit(solution)/shard_map/all_to_all | solution.py:83
  863.5 3.2 copy-start.1
Sparse Core Ops, SparseCore 0:
  31.9 55.9 reduce-scatter.7
  90.2 76.9 reduce-scatter.5
  211.8 51.1 reduce-scatter.9
  265.1 51.8 reduce-scatter.11
  319.1 59.9 reduce-scatter.13
